TPU v7x, 256 devices: a whole 4x4x8 slice. The times are simulated.
256 devices in a mesh: cfg: 2 (over z_lo), req: 16 (over y, z_hi), mlp: 8 (over x, core).
Axes of the slice: x: 4, y: 4, z: 8 (z_hi: 4, z_lo: 2; z = z_hi * 2 + z_lo), core: 2. Of those that a mesh axis runs over, the one named last changes fastest.
Arguments:
- hidden: bfloat16 [2, 16384, 1152], P('cfg', ('req', 'mlp')), may hold values from -64 to 64
- noisy_latent: float32 [16384, 16], P(('req', 'mlp'), 'cfg'), may hold values from -6 to 6
- labels: int32 [16, 4], replicated, may hold values from 0 to 999
- timesteps: int32 [16, 4], replicated, may hold values from 0 to 999
- lengths: int32 [16, 4], P('req'), may hold values from 1 to 512, 1024 in all within a row
- guidance: float32 [16, 4], P('req'), may hold values from 1.5 to 4
- keep_scale: float32 [16, 4], P('req'), may hold values from 0.9 to 1.2
- noise_scale: float32 [16, 4], P('req'), may hold values from -0.8 to -0.2
- class_table: bfloat16 [1001, 1152], replicated, may hold values from -6 to 6
- time_up: bfloat16 [256, 1152], replicated, may hold values from -0.375 to 0.375
- time_up_bias: bfloat16 [1152], replicated, may hold values from -4 to 4
- time_out: bfloat16 [1152, 1152], replicated, may hold values from -0.1875 to 0.1875
- time_out_bias: bfloat16 [1152], replicated, may hold values from -4 to 4
- mod_weight: bfloat16 [1152, 9216], P(None, 'req'), may hold values from -0.1875 to 0.1875
- mod_bias: bfloat16 [9216], P('req'), may hold values from -4 to 4
- qkv_weight: bfloat16 [1152, 3456], P(None, 'req'), may hold values from -8 to 8
- qkv_bias: bfloat16 [3456], P('req'), may hold values from -4 to 4
- out_weight: bfloat16 [1152, 1152], P(None, 'req'), may hold values from -0.1875 to 0.1875
- out_bias: bfloat16 [1152], P('req'), may hold values from -4 to 4
- up_weight: bfloat16 [1152, 4608], P(None, 'mlp'), may hold values from -0.1875 to 0.1875
- up_bias: bfloat16 [4608], P('mlp'), may hold values from -4 to 4
- down_weight: bfloat16 [4608, 1152], P('mlp'), may hold values from -1 to 1
- down_bias: bfloat16 [1152], replicated, may hold values from -4 to 4
- final_weight: bfloat16 [1152, 16], replicated, may hold values from -0.1875 to 0.1875
- final_bias: bfloat16 [16], replicated, may hold values from -4 to 4
Outputs:
- next_latent: float32 [16384, 16], P(('req', 'mlp'), 'cfg')
Inputs may be any that keep to these rules, and one draw needn't show every extreme that they name: `lengths`: each row sums to 1024, and its largest crop has exactly 512 tokens.
All inputs are finite; a program needn't handle non-finite values.
Results may differ from a plain program's by a relative error of at most 0.015.
Values may be sent and summed in bfloat16 or wider, within the bound.
No kernel may reach another device: no remote copies, remote signals or barrier semaphores. Data moves between devices by JAX's collectives and lax.ppermute only.
A program may use at most 128 MiB of HBM per device.

v0:
```python
import math
import jax
import jax.numpy as jnp
from jax import lax
from jax.sharding import PartitionSpec as P

HEADS = 16
HEAD_DIM = 72
CLASSES = 1000
FREQ = 256


def layer_norm(values):
    values = values.astype(jnp.float32)
    centre = values - jnp.mean(values, axis=-1, keepdims=True)
    variance = jnp.mean(centre * centre, axis=-1, keepdims=True)
    return centre * lax.rsqrt(variance + 1e-06)


def time_features(times_flat):
    half_freq = FREQ // 2
    frequency = jnp.exp(-math.log(10000.0) * jnp.arange(half_freq, dtype=jnp.float32) / half_freq)
    angles = times_flat.astype(jnp.float32)[:, None] * frequency[None, :]
    return jnp.concatenate([jnp.cos(angles), jnp.sin(angles)], axis=1).astype(jnp.bfloat16)


def segment_ids(lengths_row, positions):
    ends = jnp.cumsum(lengths_row)
    return jnp.sum((positions[:, None] >= ends[None, :]).astype(jnp.int32), axis=1)


def attention(queries, keys_all, values_all, query_segment, key_segment):
    scores = jnp.einsum(
        "qhd,khd->hqk", queries, keys_all, preferred_element_type=jnp.float32
    ) / math.sqrt(HEAD_DIM)
    same = (query_segment[:, None] == key_segment[None, :])[None]
    masked = jnp.where(same, scores, -1e30)
    row_max = jnp.max(masked, axis=2, keepdims=True)
    expo = jnp.where(same, jnp.exp(masked - row_max), 0.0)
    denominator = jnp.sum(expo, axis=2)
    weights = expo.astype(jnp.bfloat16)
    mixed = jnp.einsum("hqk,khd->qhd", weights, values_all, preferred_element_type=jnp.float32)
    result = mixed / jnp.transpose(denominator)[:, :, None]
    return result.astype(jnp.bfloat16).reshape(queries.shape[0], -1)


def shards(
    hidden,
    noisy_latent,
    labels,
    timesteps,
    lengths,
    guidance,
    keep_scale,
    noise_scale,
    class_table,
    time_up,
    time_up_bias,
    time_out,
    time_out_bias,
    mod_weight,
    mod_bias,
    qkv_weight,
    qkv_bias,
    out_weight,
    out_bias,
    up_weight,
    up_bias,
    down_weight,
    down_bias,
    final_weight,
    final_bias,
):
    req_count = lax.axis_size("req")
    mlp_count = lax.axis_size("mlp")
    half_index = lax.axis_index("cfg")
    mlp_index = lax.axis_index("mlp")
    tok_rows = hidden.shape[1]
    width = hidden.shape[2]
    group_rows = tok_rows * mlp_count
    per_group = labels.shape[1]
    time_feat = time_features(timesteps.reshape(-1))
    time_mid = jax.nn.silu(
        jnp.dot(time_feat, time_up, preferred_element_type=jnp.float32)
        + time_up_bias.astype(jnp.float32)
    ).astype(jnp.bfloat16)
    time_cond = jnp.dot(
        time_mid, time_out, preferred_element_type=jnp.float32
    ) + time_out_bias.astype(jnp.float32)
    used_labels = jnp.where(half_index == 0, labels.reshape(-1), CLASSES)
    one_hot = (used_labels[:, None] == jnp.arange(CLASSES + 1, dtype=jnp.int32)[None, :]).astype(
        jnp.bfloat16
    )
    cond_act = jax.nn.silu(
        time_cond + jnp.dot(one_hot, class_table, preferred_element_type=jnp.float32)
    ).astype(jnp.bfloat16)
    local_mod = (
        jnp.dot(cond_act, mod_weight, preferred_element_type=jnp.float32)
        + mod_bias.astype(jnp.float32)
    ).astype(jnp.bfloat16)
    local_mod = local_mod.reshape(req_count, per_group, local_mod.shape[1])
    modulation = lax.all_to_all(local_mod, "req", split_axis=0, concat_axis=2, tiled=True)[0]
    positions = jnp.arange(group_rows, dtype=jnp.int32)
    segment_all = segment_ids(lengths[0], positions)
    segment_own = lax.dynamic_slice_in_dim(segment_all, mlp_index * tok_rows, tok_rows)
    member = segment_own[:, None] == jnp.arange(per_group, dtype=jnp.int32)[None, :]
    per_token = jnp.dot(member.astype(jnp.bfloat16), modulation, preferred_element_type=jnp.float32)
    pieces = [per_token[:, index * width : (index + 1) * width] for index in range(8)]
    shift_attn, scale_attn, gate_attn, shift_mlp, scale_mlp, gate_mlp, shift_final, scale_final = (
        pieces
    )
    rows = hidden[0]
    normed = (layer_norm(rows) * (1.0 + scale_attn) + shift_attn).astype(jnp.bfloat16)
    qkv_full, qkv_bias_full, out_full, out_bias_full = (
        lax.all_gather(qkv_weight, "req", axis=1, tiled=True),
        lax.all_gather(qkv_bias, "req", axis=0, tiled=True),
        lax.all_gather(out_weight, "req", axis=1, tiled=True),
        lax.all_gather(out_bias, "req", axis=0, tiled=True),
    )
    qkv = (
        jnp.dot(normed, qkv_full, preferred_element_type=jnp.float32)
        + qkv_bias_full.astype(jnp.float32)
    ).astype(jnp.bfloat16)
    keys_all, values_all = (
        lax.all_gather(qkv[:, width : 2 * width], "mlp", axis=0, tiled=True),
        lax.all_gather(qkv[:, 2 * width :], "mlp", axis=0, tiled=True),
    )
    attended = attention(
        qkv[:, :width].reshape(tok_rows, HEADS, HEAD_DIM),
        keys_all.reshape(group_rows, HEADS, HEAD_DIM),
        values_all.reshape(group_rows, HEADS, HEAD_DIM),
        segment_own,
        segment_all,
    )
    projected = jnp.dot(
        attended, out_full, preferred_element_type=jnp.float32
    ) + out_bias_full.astype(jnp.float32)
    mid_hidden = (rows.astype(jnp.float32) + gate_attn * projected).astype(jnp.bfloat16)
    normed_mlp = (layer_norm(mid_hidden) * (1.0 + scale_mlp) + shift_mlp).astype(jnp.bfloat16)
    gathered = lax.all_gather(normed_mlp, "mlp", axis=0, tiled=True)
    inner = jax.nn.gelu(
        jnp.dot(gathered, up_weight, preferred_element_type=jnp.float32)
        + up_bias.astype(jnp.float32),
        approximate=True,
    ).astype(jnp.bfloat16)
    mlp_out = lax.psum_scatter(
        jnp.dot(inner, down_weight, preferred_element_type=jnp.float32).astype(jnp.bfloat16),
        "mlp",
        scatter_dimension=0,
        tiled=True,
    ).astype(jnp.float32)
    final_hidden = mid_hidden.astype(jnp.float32) + gate_mlp * (
        mlp_out + down_bias.astype(jnp.float32)
    )
    normed_final = (layer_norm(final_hidden) * (1.0 + scale_final) + shift_final).astype(
        jnp.bfloat16
    )
    predicted = jnp.dot(
        normed_final, final_weight, preferred_element_type=jnp.float32
    ) + final_bias.astype(jnp.float32)
    halves = lax.all_to_all(predicted[None], "cfg", split_axis=2, concat_axis=0, tiled=True)
    eps_cond = halves[0]
    eps_free = halves[1]
    member_f = member.astype(jnp.float32)
    guide_tok = jnp.sum(member_f * guidance, axis=1, keepdims=True)
    keep_tok = jnp.sum(member_f * keep_scale, axis=1, keepdims=True)
    noise_tok = jnp.sum(member_f * noise_scale, axis=1, keepdims=True)
    return keep_tok * noisy_latent + noise_tok * (eps_free + guide_tok * (eps_cond - eps_free))


def solution(mesh):
    return jax.shard_map(
        shards,
        mesh=mesh,
        in_specs=(
            P("cfg", ("req", "mlp"), None),
            P(("req", "mlp"), "cfg"),
            P(),
            P(),
            P("req", None),
            P("req", None),
            P("req", None),
            P("req", None),
            P(),
            P(),
            P(),
            P(),
            P(),
            P(None, "req"),
            P("req"),
            P(None, "req"),
            P("req"),
            P(None, "req"),
            P("req"),
            P(None, "mlp"),
            P("mlp"),
            P("mlp", None),
            P(),
            P(),
            P(),
        ),
        out_specs=P(("req", "mlp"), "cfg"),
        check_vma=False,
    )
```

profile of v0, /device:TPU:8, one launch (start us, length us, event | category | flops | bytes accessed | tf_op | source)
XLA Modules:
  0.0 357.1 jit_solution(16776291229437060213)
XLA Ops:
  11.4 1.8 convolution_add_fusion.3
  13.2 3.0 fusion.29
  16.9 11.6 %all-to-all-start = ((bf16[16,4,576]{2,1,0:T(4,128)(2,1)}), bf16[16,4,576]{2,1,0:T(4,128)(2,1)S(1)}, u32[]{:S(2)}, u32[]{:S(2)}) async-start(bf16[16,4,576]{2,1,0:T(4,128)(2,1)} %reshape.143), calls=%async_computation | async-start | bytes 163840 | tf_op jit(solution)/shard_map/all_to_all | solution.py:102
  31.1 82.8 %all-reduce.2 = (bf16[3456]{0:T(1024)(128)(2,1)S(1)}, bf16[1152]{0:T(1024)(128)(2,1)S(1)}) all-reduce(bf16[3456]{0:T(1024)(128)(2,1)S(1)} %dynamic-update-slice, bf16[1152]{0:T(1024)(128)(2,1)S(1)} %dynamic-update-slice.1), channel_id=1, replica_groups=mesh['cfg'=2,'req'=16,'mlp'=8] {'req'}, use_global_device_ids=true, to_apply=%add | all-reduce | flops 4608 | bytes 18432
  114.6 3.0 fusion.67
  117.6 6.1 %fusion.2 = bf16[128,3456]{1,0:T(8,128)(2,1)S(1)} fusion(bf16[1152,3456]{0,1:T(8,128)(2,1)} %all-gather.6.cloned.1.call-done, f32[3456]{0:T(1024)S(1)} %convert_element_type.103, bf16[1,128,1152]{2,1,0:T(8,128)(2,1)S(1)} %copy-done.1, f32[128,9216]{1,0:T(8,128)} %fusion.67, f32[128]{0:T(128)S(1)} %add_rsqrt_fusion.2, f32[128]{0:T(128)S(1)} %broadcast_multiply_fusion.2), kind=kOutput, calls=%fused_computation.5 | convolution fusion | flops 1021132800 | bytes 10336768 | tf_op jit(solution)/shard_map/dot_general | solution.py:121
  123.7 0.9 fusion.83
  126.2 0.8 broadcast_compare_fusion
  127.2 37.7 %all-gather.10.cloned.1.call-done = bf16[1024,1152]{1,0:T(8,128)(2,1)} async-done(((bf16[128,1152]{1,0:T(8,128)(2,1)}), bf16[1024,1152]{1,0:T(8,128)(2,1)}) %all-gather.10.cloned.1.call-update) | async-done | bytes 2359312 | tf_op jit(solution)/shard_map/all_gather | solution.py:125
  164.9 4.3 %copy.52 = bf16[1024,1152]{0,1:T(8,128)(2,1)} copy(bf16[1024,1152]{1,0:T(8,128)(2,1)} %all-gather.10.cloned.1.call-done) | data formatting | bytes 4718592 | tf_op jit(solution)/shard_map/all_gather | solution.py:125
  169.2 26.3 %all-gather.8.cloned.1.call-done = bf16[1024,1152]{1,0:T(8,128)(2,1)} async-done(((bf16[128,1152]{1,0:T(8,128)(2,1)}), bf16[1024,1152]{1,0:T(8,128)(2,1)}) %all-gather.8.cloned.1.call-update) | async-done | bytes 2359312 | tf_op jit(solution)/shard_map/all_gather | solution.py:126
  195.5 4.3 %copy.50 = bf16[1024,1152]{0,1:T(8,128)(2,1)} copy(bf16[1024,1152]{1,0:T(8,128)(2,1)} %all-gather.8.cloned.1.call-done) | data formatting | bytes 4718592 | tf_op jit(solution)/shard_map/all_gather | solution.py:126
  199.8 7.5 %fusion.84 = (f32[16,128]{1,0:T(8,128)S(1)}, bf16[16,128,1024]{2,1,0:T(8,128)(2,1)}) fusion(pred[128,1024]{1,0:T(8,128)(4,1)S(1)} %copy-done.2, bf16[128,16,72]{0,2,1:T(8,128)(2,1)S(1)} %bitcast.88, bf16[1024,16,72]{0,2,1:T(8,128)(2,1)} %bitcast.84), kind=kOutput, calls=%fused_computation.112 | convolution fusion | flops 314573824 | bytes 6987776 | tf_op jit(solution)/shard_map/sub | solution.py:39
  207.2 5.2 %fusion.26 = bf16[128,16,72]{0,2,1:T(8,128)(2,1)} fusion(bf16[1024,16,72]{0,2,1:T(8,128)(2,1)} %bitcast.85, bf16[16,128,1024]{2,1,0:T(8,128)(2,1)} %get-tuple-element.18, f32[128,16]{0,1:T(8,128)S(1)} %bitcast.95), kind=kOutput, calls=%fused_computation.31 | convolution fusion | flops 302284800 | bytes 6856704 | tf_op jit(solution)/shard_map/hqk,khd->qhd/dot_general | solution.py:42
  212.4 49.4 %all-gather.12.cloned.1.call-done = bf16[1152,1152]{0,1:T(8,128)(2,1)} async-done(((bf16[1152,72]{0,1:T(8,128)(2,1)}), bf16[1152,1152]{0,1:T(8,128)(2,1)}) %all-gather.12.cloned.1.call-update) | async-done | bytes 2654224 | tf_op jit(solution)/shard_map/all_gather | solution.py:117
  261.8 3.0 fusion.85
  265.0 2.2 fusion.41
  267.3 26.1 %all-gather.14.cloned.1.call-done = bf16[1024,1152]{1,0:T(8,128)(2,1)} async-done(((bf16[128,1152]{1,0:T(8,128)(2,1)}), bf16[1024,1152]{1,0:T(8,128)(2,1)}) %all-gather.14.cloned.1.call-update) | async-done | bytes 2359312 | tf_op jit(solution)/shard_map/all_gather | solution.py:140
  293.4 7.8 %convolution_convert_fusion = bf16[1024,1152]{1,0:T(8,128)(2,1)} fusion(bf16[576,1152]{1,0:T(8,128)(2,1)} %param.46, bf16[1024,1152]{1,0:T(8,128)(2,1)} %all-gather.14.cloned.1.call-done, bf16[1152,576]{0,1:T(8,128)(2,1)} %param.44, f32[576]{0:T(1024)S(1)} %convert_element_type.111), kind=kOutput, calls=%fused_computation.11 | convolution fusion | flops 2724986880 | bytes 7375104 | tf_op jit(solution)/shard_map/dot_general | solution.py:147
  301.9 36.9 %reduce-scatter.2.cloned.1.call-done = bf16[128,1152]{1,0:T(8,128)(2,1)} async-done(((bf16[1024,1152]{1,0:T(8,128)(2,1)}), bf16[128,1152]{1,0:T(8,128)(2,1)}) %reduce-scatter.2.cloned.1.call-update) | async-done | bytes 294928 | tf_op jit(solution)/shard_map/reduce_scatter | solution.py:146
  338.8 1.3 fusion.81
  340.4 2.2 convolution_add_fusion.6
  342.6 3.2 all-to-all-start.1
  345.9 3.7 %all-to-all-done.1 = f32[1,128,16]{1,0,2:T(1,128)S(1)} async-done(((f32[1,128,16]{1,0,2:T(1,128)}), f32[1,128,16]{1,0,2:T(1,128)S(1)}, u32[]{:S(2)}, u32[]{:S(2)}) %all-to-all-start.1) | async-done | bytes 8224 | tf_op jit(solution)/shard_map/all_to_all | solution.py:161
  (84 shorter events, 11.1 us)
Async XLA Ops:
  6.5 4.8 %copy-start = (bf16[1152,1152]{1,0:T(8,128)(2,1)S(1)}, bf16[1152,1152]{1,0:T(8,128)(2,1)}, u32[]{:S(2)}) copy-start(bf16[1152,1152]{1,0:T(8,128)(2,1)} %param.36) | copy-start | bytes 7962628
  6.5 111.0 %all-gather.6.cloned.1.call-start = ((), (), s32[]{:S(2)}) async-start(), calls=%async_computation.3 | async-start | bytes 8460288 | tf_op jit(solution)/shard_map/all_gather | solution.py:115
  13.2 15.4 %copy-start.10 = (s32[1,4]{1,0:T(1,128)S(1)}, s32[1,4]{1,0:T(1,128)}, u32[]{:S(2)}) copy-start(s32[1,4]{1,0:T(1,128)} %param.29) | copy-start | bytes 52
  13.2 15.5 %copy-start.14 = (u32[256]{0:T(256)S(1)}, u32[256]{0:T(256)}, u32[]{:S(2)}) copy-start(u32[256]{0:T(256)} %constant.70) | copy-start | bytes 3076
  13.2 17.4 %copy-start.11 = (bf16[216]{0:T(256)(128)(2,1)S(1)}, bf16[216]{0:T(256)(128)(2,1)}, u32[]{:S(2)}) copy-start(bf16[216]{0:T(256)(128)(2,1)} %param.41) | copy-start | bytes 1300
  13.2 17.7 %copy-start.12 = (bf16[72]{0:T(256)(128)(2,1)S(1)}, bf16[72]{0:T(256)(128)(2,1)}, u32[]{:S(2)}) copy-start(bf16[72]{0:T(256)(128)(2,1)} %param.43) | copy-start | bytes 436
  13.2 100.9 %copy-start.1 = (bf16[1,128,1152]{2,1,0:T(8,128)(2,1)S(1)}, bf16[1,128,1152]{2,1,0:T(8,128)(2,1)}, u32[]{:S(2)}) copy-start(bf16[1,128,1152]{2,1,0:T(8,128)(2,1)} %param.25) | copy-start | bytes 884740
  16.9 97.5 %all-to-all-start = ((bf16[16,4,576]{2,1,0:T(4,128)(2,1)}), bf16[16,4,576]{2,1,0:T(4,128)(2,1)S(1)}, u32[]{:S(2)}, u32[]{:S(2)}) async-start(bf16[16,4,576]{2,1,0:T(4,128)(2,1)} %reshape.143), calls=%async_computation | async-start | bytes 163840 | tf_op jit(solution)/shard_map/all_to_all | solution.py:102
  28.5 136.4 %all-gather.10.cloned.1.call-start = ((), (), s32[]{:S(2)}) async-start(), calls=%async_computation.5 | async-start | bytes 2654208 | tf_op jit(solution)/shard_map/all_gather | solution.py:125
  124.6 70.8 %all-gather.8.cloned.1.call-start = ((), (), s32[]{:S(2)}) async-start(), calls=%async_computation.4 | async-start | bytes 2654208 | tf_op jit(solution)/shard_map/all_gather | solution.py:126
  125.4 136.4 %all-gather.12.cloned.1.call-start = ((), (), s32[]{:S(2)}) async-start(), calls=%async_computation.6 | async-start | bytes 2820096 | tf_op jit(solution)/shard_map/all_gather | solution.py:117
  125.9 167.4 %all-gather.14.cloned.1.call-start = ((), (), s32[]{:S(2)}) async-start(), calls=%async_computation.7 | async-start | bytes 2654208 | tf_op jit(solution)/shard_map/all_gather | solution.py:140
  169.2 30.6 %copy-start.2 = (pred[128,1024]{1,0:T(8,128)(4,1)S(1)}, pred[128,1024]{1,0:T(8,128)(4,1)}, u32[]{:S(2)}) copy-start(pred[128,1024]{1,0:T(8,128)(4,1)} %broadcast_compare_fusion) | copy-start | bytes 393220
  264.8 2.5 copy-start.6
  267.2 71.7 %reduce-scatter.2.cloned.1.call-start = ((), (), s32[]{:S(2)}) async-start(), calls=%async_computation.8 | async-start | bytes 2654208 | tf_op jit(solution)/shard_map/reduce_scatter | solution.py:146
  301.2 0.7 copy-start.4
  301.2 0.7 copy-start.13
  301.2 39.2 %copy-start.3 = (bf16[1152,16]{0,1:T(8,128)(2,1)S(1)}, bf16[1152,16]{0,1:T(8,128)(2,1)}, u32[]{:S(2)}) copy-start(bf16[1152,16]{0,1:T(8,128)(2,1)} %param.48) | copy-start | bytes 110596
  301.9 43.9 %copy-start.7 = (f32[1,4]{1,0:T(1,128)S(1)}, f32[1,4]{1,0:T(1,128)}, u32[]{:S(2)}) copy-start(f32[1,4]{1,0:T(1,128)} %param.31) | copy-start | bytes 52
  301.9 44.0 %copy-start.8 = (f32[1,4]{1,0:T(1,128)S(1)}, f32[1,4]{1,0:T(1,128)}, u32[]{:S(2)}) copy-start(f32[1,4]{1,0:T(1,128)} %param.30) | copy-start | bytes 52
  301.9 44.0 %copy-start.9 = (f32[1,4]{1,0:T(1,128)S(1)}, f32[1,4]{1,0:T(1,128)}, u32[]{:S(2)}) copy-start(f32[1,4]{1,0:T(1,128)} %param.32) | copy-start | bytes 52
  301.9 47.7 %copy-start.5 = (f32[128,8]{0,1:T(8,128)S(1)}, f32[128,8]{0,1:T(8,128)}, u32[]{:S(2)}) copy-start(f32[128,8]{0,1:T(8,128)} %param.26) | copy-start | bytes 12292
  342.6 7.0 %all-to-all-start.1 = ((f32[1,128,16]{1,0,2:T(1,128)}), f32[1,128,16]{1,0,2:T(1,128)S(1)}, u32[]{:S(2)}, u32[]{:S(2)}) async-start(f32[1,128,16]{1,0,2:T(1,128)} %bitcast.16), calls=%async_computation.2 | async-start | bytes 16384 | tf_op jit(solution)/shard_map/all_to_all | solution.py:161
Sparse Core Ops, SparseCore 0:
  9.8 107.0 all-gather.5
  124.8 40.0 all-gather.9
  166.7 28.6 all-gather.7
  197.8 63.9 all-gather.11
  267.3 26.0 all-gather.13
  301.3 37.4 reduce-scatter.1
where the time goes:
time: 358 us; the launch traced here: 357 us
  waiting for transfers between devices  182 us (51%)
  blocking collectives  82.8 us (23%)
  matrix products  39.5 us (11%)
  starting transfers between devices  15.2 us (4%)
  between operations  15 us (4%)
  local copies, waits for them, and re-layouts  12.7 us (4%)
  other arithmetic  9.78 us (3%)
    unnamed x1, blocking collectives  82.8 us
    all_gather x1, waiting for transfers between devices, shards(): lax.all_gather(out_weight, 'req', axis=1, tiled=True)  49.4 us
    all_gather x1, waiting for transfers between devices, shards(): lax.all_gather(qkv[:, width:2 * width], 'mlp', axis=0, tiled=True)  37.7 us
    reduce_scatter x1, waiting for transfers between devices, shards(): lax.psum_scatter(jnp.dot(inner, down_weight, preferred_element_type=jnp.f...  36.9 us
    all_gather x1, waiting for transfers between devices, shards(): lax.all_gather(qkv[:, 2 * width:], 'mlp', axis=0, tiled=True)  26.3 us
    all_gather x1, waiting for transfers between devices, shards(): gathered = lax.all_gather(normed_mlp, 'mlp', axis=0, tiled=True)  26.1 us
    all_to_all x1, starting transfers between devices, shards(): lax.all_to_all(local_mod, 'req', split_axis=0, concat_axis=2, tiled=True)[0]  11.6 us
    dot_general x1, matrix products, shards(): jnp.dot(inner, down_weight, preferred_element_type=jnp.float32)  7.81 us
  transfers between devices with their start and end apart: 8, of which 6 were waited for; matrix products, arithmetic and copies ran while one was open for 10% of the time, Pallas kernels for 0%

commit v1 on v0

--- a/solution.py
+++ b/solution.py
@@ -8,6 +8,27 @@
 HEAD_DIM = 72
 CLASSES = 1000
 FREQ = 256
+
+
+def ring_gather(shard, axis, dim):
+    length, here, rows = (lax.axis_size(axis), lax.axis_index(axis), shard.shape[dim])
+    right = [(i, (i + 1) % length) for i in range(length)]
+    backward = [(i, (i - 1) % length) for i in range(length)]
+    whole = jnp.zeros((*shard.shape[:dim], length * rows, *shard.shape[dim + 1 :]), shard.dtype)
+    whole = lax.dynamic_update_slice_in_dim(whole, shard, here * rows, axis=dim)
+    from_left = from_right = shard
+    half = length // 2
+    for step in range(1, half + 1):
+        from_left = lax.ppermute(from_left, axis, right)
+        whole = lax.dynamic_update_slice_in_dim(
+            whole, from_left, (here - step) % length * rows, axis=dim
+        )
+        if step < length - half:
+            from_right = lax.ppermute(from_right, axis, backward)
+            whole = lax.dynamic_update_slice_in_dim(
+                whole, from_right, (here + step) % length * rows, axis=dim
+            )
+    return whole
 
 
 def layer_norm(values):
@@ -123,7 +144,7 @@
     ).astype(jnp.bfloat16)
     keys_all, values_all = (
         lax.all_gather(qkv[:, width : 2 * width], "mlp", axis=0, tiled=True),
-        lax.all_gather(qkv[:, 2 * width :], "mlp", axis=0, tiled=True),
+        ring_gather(qkv[:, 2 * width :], "mlp", 0),
     )
     attended = attention(
         qkv[:, :width].reshape(tok_rows, HEADS, HEAD_DIM),

time: 358 us -> 329 us (0.919)
  waiting for transfers between devices: 182 us -> 132 us
  local copies, waits for them, and re-layouts: 12.7 us -> 25 us
  starting transfers between devices: 15.2 us -> 24.2 us
    all_gather x1, waiting for transfers between devices: 37.7 us -> 0.01 us  [shards(): lax.all_gather(qkv[:, width:2 * width], 'mlp', axis=0, tiled=True)]
    all_gather x1 -> x0, waiting for transfers between devices: 26.3 us -> none  [shards(): lax.all_gather(qkv[:, 2 * width:], 'mlp', axis=0, tiled=True)]
    ppermute x0 -> x7, waiting for transfers between devices: none -> 15.1 us  [the longest x4 12.8 us: ring_gather(): from_left = lax.ppermute(from_left, axis, right)]
    ppermute x0 -> x7, starting transfers between devices: none -> 8.89 us  [the longest x3 8.83 us: ring_gather(): from_right = lax.ppermute(from_right, axis, backward)]
    ppermute x0 -> x7, local copies, waits for them, and re-layouts: none -> 7.2 us  [the longest x4 4.66 us: ring_gather(): from_left = lax.ppermute(from_left, axis, right)]
    dynamic_update_slice x0 -> x8, local copies, waits for them, and re-layouts: none -> 6.15 us  [the longest x4 3.12 us: ring_gather(): lax.dynamic_update_slice_in_dim(whole, from_left, (here - step) % length...]
    all_gather x1 -> x0, local copies, waits for them, and re-layouts: 4.29 us -> none  [shards(): lax.all_gather(qkv[:, 2 * width:], 'mlp', axis=0, tiled=True)]
  transfers between devices with their start and end apart: 8 -> 14, of which waited for: 6 -> 8; matrix products, arithmetic and copies ran while one was open for 10% -> 15% of each run, Pallas kernels for 0% -> 0%
where the time goes in v1:
time: 329 us; the launch traced here: 328 us
  waiting for transfers between devices  132 us (40%)
  blocking collectives  82.8 us (25%)
  matrix products  39.6 us (12%)
  local copies, waits for them, and re-layouts  25 us (8%)
  starting transfers between devices  24.2 us (7%)
  between operations  14.7 us (4%)
  other arithmetic  9.78 us (3%)
    unnamed x1, blocking collectives  82.8 us
    all_gather x1, waiting for transfers between devices, shards(): lax.all_gather(out_weight, 'req', axis=1, tiled=True)  48.5 us
    reduce_scatter x1, waiting for transfers between devices, shards(): lax.psum_scatter(jnp.dot(inner, down_weight, preferred_element_type=jnp.f...  37 us
    all_gather x1, waiting for transfers between devices, shards(): gathered = lax.all_gather(normed_mlp, 'mlp', axis=0, tiled=True)  25.9 us
    ppermute x4, waiting for transfers between devices, ring_gather(): from_left = lax.ppermute(from_left, axis, right)  12.8 us
    all_to_all x1, starting transfers between devices, shards(): lax.all_to_all(local_mod, 'req', split_axis=0, concat_axis=2, tiled=True)[0]  11.6 us
    ppermute x3, starting transfers between devices, ring_gather(): from_right = lax.ppermute(from_right, axis, backward)  8.83 us
    dot_general x1, matrix products, shards(): jnp.dot(inner, down_weight, preferred_element_type=jnp.float32)  7.84 us
  transfers between devices with their start and end apart: 14, of which 8 were waited for; matrix products, arithmetic and copies ran while one was open for 15% of the time, Pallas kernels for 0%

profile of v1, /device:TPU:8, one launch (start us, length us, event | category | flops | bytes accessed | tf_op | source)
XLA Modules:
  0.0 327.7 jit_solution(4099172147767852730)
XLA Ops:
  13.2 3.0 fusion.29
  16.9 11.6 %all-to-all-start = ((bf16[16,4,576]{2,1,0:T(4,128)(2,1)}), bf16[16,4,576]{2,1,0:T(4,128)(2,1)S(1)}, u32[]{:S(2)}, u32[]{:S(2)}) async-start(bf16[16,4,576]{2,1,0:T(4,128)(2,1)} %reshape.143), calls=%async_computation | async-start | bytes 163840 | tf_op jit(solution)/shard_map/all_to_all | solution.py:123
  31.1 82.8 %all-reduce.2 = (bf16[3456]{0:T(1024)(128)(2,1)S(1)}, bf16[1152]{0:T(1024)(128)(2,1)S(1)}) all-reduce(bf16[3456]{0:T(1024)(128)(2,1)S(1)} %dynamic-update-slice, bf16[1152]{0:T(1024)(128)(2,1)S(1)} %dynamic-update-slice.1), channel_id=1, replica_groups=mesh['cfg'=2,'req'=16,'mlp'=8] {'req'}, use_global_device_ids=true, to_apply=%add | all-reduce | flops 4608 | bytes 18432
  114.6 3.0 fusion.67
  117.6 6.1 %fusion.2 = bf16[128,3456]{1,0:T(8,128)(2,1)S(1)} fusion(bf16[1152,3456]{0,1:T(8,128)(2,1)} %all-gather.5.cloned.1.call-done, f32[3456]{0:T(1024)S(1)} %convert_element_type.103, bf16[1,128,1152]{2,1,0:T(8,128)(2,1)S(1)} %copy-done.1, f32[128,9216]{1,0:T(8,128)} %fusion.67, f32[128]{0:T(128)S(1)} %add_rsqrt_fusion.2, f32[128]{0:T(128)S(1)} %broadcast_multiply_fusion.2), kind=kOutput, calls=%fused_computation.5 | convolution fusion | flops 1021132800 | bytes 10336768 | tf_op jit(solution)/shard_map/dot_general | solution.py:142
  127.2 2.9 collective-permute-start.1
  136.6 3.0 collective-permute-start.3
  140.4 1.9 collective-permute-done.2
  144.6 2.9 collective-permute-start.5
  148.2 3.0 collective-permute-done.4
  153.1 2.3 collective-permute-done.5
  157.4 7.8 %collective-permute-done.6 = bf16[128,1152]{1,0:T(8,128)(2,1)} collective-permute-done((bf16[128,1152]{1,0:T(8,128)(2,1)}, bf16[128,1152]{1,0:T(8,128)(2,1)}, u32[]{:S(2)}, u32[]{:S(2)}) %collective-permute-start.6) | collective-permute-done | bytes 294944 | tf_op jit(solution)/shard_map/ppermute | solution.py:22
  167.2 4.3 %copy.80 = bf16[1024,1152]{0,1:T(8,128)(2,1)} copy(bf16[1024,1152]{1,0:T(8,128)(2,1)} %all-gather.7.cloned.1.call-done) | data formatting | bytes 4718592 | tf_op jit(solution)/shard_map/all_gather | solution.py:146
  171.5 7.5 %fusion.84 = (f32[16,128]{1,0:T(8,128)S(1)}, bf16[16,128,1024]{2,1,0:T(8,128)(2,1)}) fusion(pred[128,1024]{1,0:T(8,128)(4,1)S(1)} %copy-done.4, bf16[128,16,72]{0,2,1:T(8,128)(2,1)S(1)} %bitcast.87, bf16[1024,16,72]{0,2,1:T(8,128)(2,1)} %bitcast.84), kind=kOutput, calls=%fused_computation.120 | convolution fusion | flops 314573824 | bytes 6987776 | tf_op jit(solution)/shard_map/sub | solution.py:60
  179.0 5.3 %fusion.26 = bf16[128,16,72]{0,2,1:T(8,128)(2,1)} fusion(bf16[1024,16,72]{0,2,1:T(8,128)(2,1)} %bitcast.8, bf16[16,128,1024]{2,1,0:T(8,128)(2,1)} %get-tuple-element.18, f32[128,16]{0,1:T(8,128)S(1)} %bitcast.94), kind=kOutput, calls=%fused_computation.31 | convolution fusion | flops 302284800 | bytes 6856704 | tf_op jit(solution)/shard_map/hqk,khd->qhd/dot_general | solution.py:63
  184.2 48.5 %all-gather.9.cloned.1.call-done = bf16[1152,1152]{0,1:T(8,128)(2,1)} async-done(((bf16[1152,72]{0,1:T(8,128)(2,1)}), bf16[1152,1152]{0,1:T(8,128)(2,1)}) %all-gather.9.cloned.1.call-update) | async-done | bytes 2654224 | tf_op jit(solution)/shard_map/all_gather | solution.py:138
  232.7 3.0 fusion.85
  235.9 2.2 fusion.41
  238.4 25.9 %all-gather.11.cloned.1.call-done = bf16[1024,1152]{1,0:T(8,128)(2,1)} async-done(((bf16[128,1152]{1,0:T(8,128)(2,1)}), bf16[1024,1152]{1,0:T(8,128)(2,1)}) %all-gather.11.cloned.1.call-update) | async-done | bytes 2359312 | tf_op jit(solution)/shard_map/all_gather | solution.py:161
  264.3 7.8 %convolution_convert_fusion = bf16[1024,1152]{1,0:T(8,128)(2,1)} fusion(bf16[576,1152]{1,0:T(8,128)(2,1)} %param.46, bf16[1024,1152]{1,0:T(8,128)(2,1)} %all-gather.11.cloned.1.call-done, bf16[1152,576]{0,1:T(8,128)(2,1)} %param.44, f32[576]{0:T(1024)S(1)} %convert_element_type.111), kind=kOutput, calls=%fused_computation.11 | convolution fusion | flops 2724986880 | bytes 7375104 | tf_op jit(solution)/shard_map/dot_general | solution.py:168
  272.8 37.0 %reduce-scatter.2.cloned.1.call-done = bf16[128,1152]{1,0:T(8,128)(2,1)} async-done(((bf16[1024,1152]{1,0:T(8,128)(2,1)}), bf16[128,1152]{1,0:T(8,128)(2,1)}) %reduce-scatter.2.cloned.1.call-update) | async-done | bytes 294928 | tf_op jit(solution)/shard_map/reduce_scatter | solution.py:167
  311.4 2.2 convolution_add_fusion.6
  313.6 3.2 all-to-all-start.1
  316.9 3.7 %all-to-all-done.1 = f32[1,128,16]{1,0,2:T(1,128)S(1)} async-done(((f32[1,128,16]{1,0,2:T(1,128)}), f32[1,128,16]{1,0,2:T(1,128)S(1)}, u32[]{:S(2)}, u32[]{:S(2)}) %all-to-all-start.1) | async-done | bytes 8224 | tf_op jit(solution)/shard_map/all_to_all | solution.py:182
  (115 shorter events, 32.2 us)
Async XLA Ops:
  6.5 111.0 %all-gather.5.cloned.1.call-start = ((), (), s32[]{:S(2)}) async-start(), calls=%async_computation.3 | async-start | bytes 8460288 | tf_op jit(solution)/shard_map/all_gather | solution.py:136
  13.2 15.4 %copy-start.12 = (s32[1,4]{1,0:T(1,128)S(1)}, s32[1,4]{1,0:T(1,128)}, u32[]{:S(2)}) copy-start(s32[1,4]{1,0:T(1,128)} %param.29) | copy-start | bytes 52
  13.2 15.5 %copy-start.16 = (u32[256]{0:T(256)S(1)}, u32[256]{0:T(256)}, u32[]{:S(2)}) copy-start(u32[256]{0:T(256)} %constant.123) | copy-start | bytes 3076
  13.2 17.4 %copy-start.13 = (bf16[216]{0:T(256)(128)(2,1)S(1)}, bf16[216]{0:T(256)(128)(2,1)}, u32[]{:S(2)}) copy-start(bf16[216]{0:T(256)(128)(2,1)} %param.41) | copy-start | bytes 1300
  13.2 17.7 %copy-start.14 = (bf16[72]{0:T(256)(128)(2,1)S(1)}, bf16[72]{0:T(256)(128)(2,1)}, u32[]{:S(2)}) copy-start(bf16[72]{0:T(256)(128)(2,1)} %param.43) | copy-start | bytes 436
  13.2 100.9 %copy-start.1 = (bf16[1,128,1152]{2,1,0:T(8,128)(2,1)S(1)}, bf16[1,128,1152]{2,1,0:T(8,128)(2,1)}, u32[]{:S(2)}) copy-start(bf16[1,128,1152]{2,1,0:T(8,128)(2,1)} %param.25) | copy-start | bytes 884740
  16.9 97.5 %all-to-all-start = ((bf16[16,4,576]{2,1,0:T(4,128)(2,1)}), bf16[16,4,576]{2,1,0:T(4,128)(2,1)S(1)}, u32[]{:S(2)}, u32[]{:S(2)}) async-start(bf16[16,4,576]{2,1,0:T(4,128)(2,1)} %reshape.143), calls=%async_computation | async-start | bytes 163840 | tf_op jit(solution)/shard_map/all_to_all | solution.py:123
  28.5 138.7 %all-gather.7.cloned.1.call-start = ((), (), s32[]{:S(2)}) async-start(), calls=%async_computation.4 | async-start | bytes 2654208 | tf_op jit(solution)/shard_map/all_gather | solution.py:146
  124.5 108.1 %all-gather.9.cloned.1.call-start = ((), (), s32[]{:S(2)}) async-start(), calls=%async_computation.5 | async-start | bytes 2820096 | tf_op jit(solution)/shard_map/all_gather | solution.py:138
  125.3 139.0 %all-gather.11.cloned.1.call-start = ((), (), s32[]{:S(2)}) async-start(), calls=%async_computation.6 | async-start | bytes 2654208 | tf_op jit(solution)/shard_map/all_gather | solution.py:161
  125.5 8.0 %collective-permute-start = (bf16[128,1152]{1,0:T(8,128)(2,1)S(1)}, bf16[128,1152]{1,0:T(8,128)(2,1)}, u32[]{:S(2)}, u32[]{:S(2)}) collective-permute-start(bf16[128,1152]{1,0:T(8,128)(2,1)S(1)} %get-tuple-element.14), channel_id=1, source_target_pairs={{0,1},{1,2},{2,3},{3,4},{4,5},{5,6},{6,7},{7,0},{8,9},{9,10},{10,1... | collective-permute-start | bytes 884744 | tf_op jit(solution)/shard_map/ppermute | solution.py:22
  127.2 8.2 %collective-permute-start.1 = (bf16[128,1152]{1,0:T(8,128)(2,1)S(1)}, bf16[128,1152]{1,0:T(8,128)(2,1)}, u32[]{:S(2)}, u32[]{:S(2)}) collective-permute-start(bf16[128,1152]{1,0:T(8,128)(2,1)S(1)} %get-tuple-element.14), channel_id=1, source_target_pairs={{0,7},{1,0},{2,1},{3,2},{4,3},{5,4},{6,5},{7,6},{8,15},{9,8},{10,9... | collective-permute-start | bytes 884744 | tf_op jit(solution)/shard_map/ppermute | solution.py:27
  134.7 7.7 %collective-permute-start.2 = (bf16[128,1152]{1,0:T(8,128)(2,1)}, bf16[128,1152]{1,0:T(8,128)(2,1)}, u32[]{:S(2)}, u32[]{:S(2)}) collective-permute-start(bf16[128,1152]{1,0:T(8,128)(2,1)} %collective-permute-done), channel_id=1, source_target_pairs={{0,1},{1,2},{2,3},{3,4},{4,5},{5,6},{6,7},{7,0},{8,9},{9,10},{10,1... | collective-permute-start | bytes 884744 | tf_op jit(solution)/shard_map/ppermute | solution.py:22
  136.6 7.7 %collective-permute-start.3 = (bf16[128,1152]{1,0:T(8,128)(2,1)}, bf16[128,1152]{1,0:T(8,128)(2,1)S(1)}, u32[]{:S(2)}, u32[]{:S(2)}) collective-permute-start(bf16[128,1152]{1,0:T(8,128)(2,1)} %collective-permute-done.1), channel_id=1, source_target_pairs={{0,7},{1,0},{2,1},{3,2},{4,3},{5,4},{6,5},{7,6},{8,15},{9,8},{10,9... | collective-permute-start | bytes 884744 | tf_op jit(solution)/shard_map/ppermute | solution.py:27
  143.5 7.7 %collective-permute-start.4 = (bf16[128,1152]{1,0:T(8,128)(2,1)}, bf16[128,1152]{1,0:T(8,128)(2,1)}, u32[]{:S(2)}, u32[]{:S(2)}) collective-permute-start(bf16[128,1152]{1,0:T(8,128)(2,1)} %collective-permute-done.2), channel_id=1, source_target_pairs={{0,1},{1,2},{2,3},{3,4},{4,5},{5,6},{6,7},{7,0},{8,9},{9,10},{10,1... | collective-permute-start | bytes 884744 | tf_op jit(solution)/shard_map/ppermute | solution.py:22
  144.6 10.9 %collective-permute-start.5 = (bf16[128,1152]{1,0:T(8,128)(2,1)S(1)}, bf16[128,1152]{1,0:T(8,128)(2,1)}, u32[]{:S(2)}, u32[]{:S(2)}) collective-permute-start(bf16[128,1152]{1,0:T(8,128)(2,1)S(1)} %collective-permute-done.3), channel_id=1, source_target_pairs={{0,7},{1,0},{2,1},{3,2},{4,3},{5,4},{6,5},{7,6},{8,15},{9,8},{10,9... | collective-permute-start | bytes 884744 | tf_op jit(solution)/shard_map/ppermute | solution.py:27
  152.4 12.9 %collective-permute-start.6 = (bf16[128,1152]{1,0:T(8,128)(2,1)}, bf16[128,1152]{1,0:T(8,128)(2,1)}, u32[]{:S(2)}, u32[]{:S(2)}) collective-permute-start(bf16[128,1152]{1,0:T(8,128)(2,1)} %collective-permute-done.4), channel_id=1, source_target_pairs={{0,1},{1,2},{2,3},{3,4},{4,5},{5,6},{6,7},{7,0},{8,9},{9,10},{10,1... | collective-permute-start | bytes 884744 | tf_op jit(solution)/shard_map/ppermute | solution.py:22
  238.1 71.7 %reduce-scatter.2.cloned.1.call-start = ((), (), s32[]{:S(2)}) async-start(), calls=%async_computation.7 | async-start | bytes 2654208 | tf_op jit(solution)/shard_map/reduce_scatter | solution.py:167
  272.1 39.3 %copy-start.5 = (bf16[1152,16]{0,1:T(8,128)(2,1)S(1)}, bf16[1152,16]{0,1:T(8,128)(2,1)}, u32[]{:S(2)}) copy-start(bf16[1152,16]{0,1:T(8,128)(2,1)} %param.48) | copy-start | bytes 110596
  272.8 44.0 %copy-start.9 = (f32[1,4]{1,0:T(1,128)S(1)}, f32[1,4]{1,0:T(1,128)}, u32[]{:S(2)}) copy-start(f32[1,4]{1,0:T(1,128)} %param.31) | copy-start | bytes 52
  272.8 44.0 %copy-start.10 = (f32[1,4]{1,0:T(1,128)S(1)}, f32[1,4]{1,0:T(1,128)}, u32[]{:S(2)}) copy-start(f32[1,4]{1,0:T(1,128)} %param.30) | copy-start | bytes 52
  272.8 44.0 %copy-start.11 = (f32[1,4]{1,0:T(1,128)S(1)}, f32[1,4]{1,0:T(1,128)}, u32[]{:S(2)}) copy-start(f32[1,4]{1,0:T(1,128)} %param.32) | copy-start | bytes 52
  272.8 47.8 %copy-start.7 = (f32[128,8]{0,1:T(8,128)S(1)}, f32[128,8]{0,1:T(8,128)}, u32[]{:S(2)}) copy-start(f32[128,8]{0,1:T(8,128)} %param.26) | copy-start | bytes 12292
  313.6 7.0 %all-to-all-start.1 = ((f32[1,128,16]{1,0,2:T(1,128)}), f32[1,128,16]{1,0,2:T(1,128)S(1)}, u32[]{:S(2)}, u32[]{:S(2)}) async-start(f32[1,128,16]{1,0,2:T(1,128)} %bitcast.16), calls=%async_computation.2 | async-start | bytes 16384 | tf_op jit(solution)/shard_map/all_to_all | solution.py:182
  (7 other events, 22.2 us)
Sparse Core Ops, SparseCore 0:
  9.8 105.5 all-gather.4
  124.7 42.0 all-gather.6
  169.3 63.3 all-gather.8
  238.2 26.0 all-gather.10
  272.3 37.5 reduce-scatter.1
